TPU v7x, 32 devices: a whole 2x2x4 slice. The times are simulated.
32 devices in a mesh: groups: 2 (over y), seq: 4 (over z), tensor: 2 (over x), dp: 2 (over core).
Axes of the slice: x: 2, y: 2, z: 4, core: 2. Of those that a mesh axis runs over, the one named last changes fastest.
Arguments:
- tokens: bfloat16 [4, 1024, 4096], P(('groups', 'dp'), 'seq', 'tensor'), parts along dimension 0, may hold values from -6 to 6
- doc_lengths: int32 [4, 8], P(('groups', 'dp')), parts along dimension 0, may hold values from 1 to 768, 1024 in all within a row
- low_taps: float32 [2, 4096], P(None, 'tensor'), may hold values from 0.66 to 0.75
- high_taps: float32 [2, 4096], P(None, 'tensor'), may hold values from -2.5 to 2.5
- level_weights: float32 [13, 4096], P(None, 'tensor'), may hold values from -2.5 to 2.5
- mix_weight: bfloat16 [4096, 4096], P(None, 'tensor'), may hold values from -0.09375 to 0.09375
- out_grad: bfloat16 [4, 1024, 4096], P(('groups', 'dp'), 'seq', 'tensor'), parts along dimension 0, may hold values from -6 to 6
Outputs:
- result: bfloat16 [4, 1024, 4096], P(('groups', 'dp'), 'seq', 'tensor'), parts along dimension 0
- token_grad: bfloat16 [4, 1024, 4096], P(('groups', 'dp'), 'seq', 'tensor'), parts along dimension 0
- weight_grad: bfloat16 [8192, 4096], P(('groups', 'seq', 'dp'), 'tensor'), parts along dimension 0
- low_grad: float32 [4, 4096], P('groups', 'tensor'), parts along dimension 0
- high_grad: float32 [4, 4096], P('groups', 'tensor'), parts along dimension 0
- level_grad: float32 [26, 4096], P('groups', 'tensor'), parts along dimension 0
There are 2 independent parts, one for each index of `groups`. A program takes and returns all parts, laid end to end along the dimension named above; an argument that names none is the same for every part. Nothing has to cross between parts.
Inputs may be any that keep to these rules, and one draw needn't show every extreme that they name: `doc_lengths`: each row of 8 lengths sums to 1024, and its longest document has exactly 768 positions.
All inputs are finite; a program needn't handle non-finite values.
Results may differ from a plain program's by a relative error of at most 0.015.
Values may be sent and summed in bfloat16 or wider, within the bound.
No kernel may reach another device: no remote copies, remote signals or barrier semaphores. Data moves between devices by JAX's collectives and lax.ppermute only.
A program may use at most 128 MiB of HBM per device.

v0:
```python
import jax
import jax.numpy as jnp
from jax import lax
from jax.sharding import PartitionSpec as P

GELU_SCALE = 0.7978845608028654
GELU_CUBIC = 0.044715


def shifted_2(block, axis, distance):
    devices = range(lax.axis_size(axis))
    route = [(i - distance, i) for i in devices if i - distance in devices]
    return lax.ppermute(block, axis, route)


def gelu_value(values):
    tangent = jnp.tanh(GELU_SCALE * (values + GELU_CUBIC * values * values * values))
    return 0.5 * values * (1.0 + tangent)


def gelu_slope(values):
    tangent = jnp.tanh(GELU_SCALE * (values + GELU_CUBIC * values * values * values))
    return 0.5 * (1.0 + tangent) + 0.5 * values * (1.0 - tangent * tangent) * GELU_SCALE * (
        1.0 + 3.0 * GELU_CUBIC * values * values
    )


def doc_starts(positions, doc_lengths):
    bounds = jnp.cumsum(doc_lengths, axis=1) - doc_lengths
    before = bounds[:, None, :] <= positions[None, :, None]
    return jnp.max(jnp.where(before, bounds[:, None, :], -1), axis=2)


def tap_mask(positions, starts, spacing):
    return (positions[None, :] - spacing >= starts)[:, :, None]


def shards(tokens, doc_lengths, low_taps, high_taps, level_weights, mix_weight, out_grad):
    batch_size, row_count, channels = tokens.shape
    levels = level_weights.shape[0] - 1
    seq_count = lax.axis_size("seq")
    core_count = lax.axis_size("dp")
    grad_scale = float(batch_size * row_count * seq_count * core_count) ** (-0.5)
    offset = lax.axis_index("seq") * row_count
    positions = offset + jnp.arange(row_count, dtype=jnp.int32)
    starts = doc_starts(positions, doc_lengths)
    shallow = min(levels, row_count.bit_length() - 1)
    summed = jnp.zeros(tokens.shape, jnp.float32)
    states = [tokens]
    previous_list = []
    current = tokens
    for level_index in range(shallow):
        spacing = 2**level_index
        border = shifted_2(current[:, row_count - spacing :, :], "seq", 1)
        shifted = jnp.concatenate([border, current[:, : row_count - spacing, :]], axis=1)
        previous = jnp.where(tap_mask(positions, starts, spacing), shifted, jnp.zeros_like(shifted))
        summed = summed + level_weights[level_index] * (
            high_taps[0] * previous + high_taps[1] * current
        )
        current = (low_taps[0] * previous + low_taps[1] * current).astype(jnp.bfloat16)
        previous_list.append(previous)
        states.append(current)
    for level_index in range(shallow, levels):
        spacing = 2**level_index
        device_hops = spacing // row_count
        if device_hops < seq_count:
            shifted = shifted_2(current, "seq", device_hops)
        else:
            shifted = jnp.zeros_like(current)
        previous = jnp.where(tap_mask(positions, starts, spacing), shifted, jnp.zeros_like(shifted))
        summed = summed + level_weights[level_index] * (
            high_taps[0] * previous + high_taps[1] * current
        )
        current = (low_taps[0] * previous + low_taps[1] * current).astype(jnp.bfloat16)
        previous_list.append(previous)
        states.append(current)
    summed = summed + level_weights[levels] * current
    activated = gelu_value(summed).astype(jnp.bfloat16)
    partial_mix = jnp.einsum(
        "brc,oc->bro", activated, mix_weight, preferred_element_type=jnp.float32
    )
    mixed = lax.psum_scatter(
        partial_mix.astype(jnp.bfloat16), "tensor", scatter_dimension=2, tiled=True
    ).astype(jnp.float32)
    result = (tokens.astype(jnp.float32) + mixed).astype(jnp.bfloat16)
    gathered = lax.all_gather(out_grad, "tensor", axis=2, tiled=True)
    act_grad = jnp.einsum("bro,oc->brc", gathered, mix_weight, preferred_element_type=jnp.float32)
    weight_grad = lax.psum_scatter(
        (
            jnp.einsum("bro,brc->oc", gathered, activated, preferred_element_type=jnp.float32)
            * grad_scale
        ).astype(jnp.bfloat16),
        ("seq", "dp"),
        scatter_dimension=0,
        tiled=True,
    )
    summed_grad = act_grad * gelu_slope(summed)
    carry_grad = (level_weights[levels] * summed_grad).astype(jnp.bfloat16)
    weight_sums = [None] * (levels + 1)
    weight_sums[levels] = jnp.sum(summed_grad * states[levels].astype(jnp.float32), axis=(0, 1))
    low_first = jnp.zeros((channels,), jnp.float32)
    low_second = jnp.zeros((channels,), jnp.float32)
    high_first = jnp.zeros((channels,), jnp.float32)
    high_second = jnp.zeros((channels,), jnp.float32)
    for level_index in range(levels - 1, -1, -1):
        spacing = 2**level_index
        current = states[level_index]
        previous = previous_list[level_index]
        weighted = level_weights[level_index] * summed_grad
        highpass = high_taps[0] * previous + high_taps[1] * current
        weight_sums[level_index] = jnp.sum(summed_grad * highpass, axis=(0, 1))
        grad_wide = carry_grad.astype(jnp.float32)
        low_first = low_first + jnp.sum(grad_wide * previous.astype(jnp.float32), axis=(0, 1))
        low_second = low_second + jnp.sum(grad_wide * current.astype(jnp.float32), axis=(0, 1))
        high_first = high_first + jnp.sum(weighted * previous.astype(jnp.float32), axis=(0, 1))
        high_second = high_second + jnp.sum(weighted * current.astype(jnp.float32), axis=(0, 1))
        carried = low_taps[0] * carry_grad + high_taps[0] * weighted
        stayed = low_taps[1] * carry_grad + high_taps[1] * weighted
        outgoing = jnp.where(
            tap_mask(positions, starts, spacing), carried, jnp.zeros_like(carried)
        ).astype(jnp.bfloat16)
        if level_index < shallow:
            border = shifted_2(outgoing[:, :spacing, :], "seq", -1)
            pulled = jnp.concatenate([outgoing[:, spacing:, :], border], axis=1)
        else:
            device_hops = spacing // row_count
            if device_hops < seq_count:
                pulled = shifted_2(outgoing, "seq", -device_hops)
            else:
                pulled = jnp.zeros_like(outgoing)
        carry_grad = (stayed + pulled).astype(jnp.bfloat16)
    token_grad = (out_grad.astype(jnp.float32) + carry_grad.astype(jnp.float32)).astype(
        jnp.bfloat16
    )
    low_grad = jnp.stack([low_first, low_second]) * grad_scale
    high_grad = jnp.stack([high_first, high_second]) * grad_scale
    level_grad = jnp.stack(weight_sums) * grad_scale
    low_grad, high_grad, level_grad = (
        lax.psum(low_grad.astype(jnp.bfloat16), ("seq", "dp")).astype(jnp.float32),
        lax.psum(high_grad.astype(jnp.bfloat16), ("seq", "dp")).astype(jnp.float32),
        lax.psum(level_grad.astype(jnp.bfloat16), ("seq", "dp")).astype(jnp.float32),
    )
    return (result, token_grad, weight_grad, low_grad, high_grad, level_grad)


def solution(mesh):
    placed = (
        P(("groups", "dp"), "seq", "tensor"),
        P(("groups", "dp"), None),
        P(None, "tensor"),
        P(None, "tensor"),
        P(None, "tensor"),
        P(None, "tensor"),
        P(("groups", "dp"), "seq", "tensor"),
    )
    return jax.shard_map(
        shards,
        mesh=mesh,
        in_specs=placed,
        out_specs=(
            P(("groups", "dp"), "seq", "tensor"),
            P(("groups", "dp"), "seq", "tensor"),
            P(("groups", "seq", "dp"), "tensor"),
            P("groups", "tensor"),
            P("groups", "tensor"),
            P("groups", "tensor"),
        ),
        check_vma=False,
    )
```

profile of v0, /device:TPU:0, one launch (start us, length us, event | category | flops | bytes accessed | tf_op | source)
XLA Modules:
  0.0 565.9 jit_solution(1448448901782919432)
XLA Ops:
  8.0 4.9 collective-permute-start
  16.0 2.2 fusion.18
  18.3 3.5 collective-permute-start.1
  21.8 1.3 collective-permute-done.1
  23.9 4.2 collective-permute-start.2
  28.1 1.4 collective-permute-done.2
  30.2 4.2 collective-permute-start.3
  34.5 1.5 collective-permute-done.3
  36.7 4.2 collective-permute-start.4
  41.0 1.8 collective-permute-done.4
  43.4 4.3 collective-permute-start.5
  47.7 3.5 collective-permute-done.5
  51.8 4.4 collective-permute-start.6
  56.3 6.0 %collective-permute-done.6 = bf16[1,64,2048]{2,1,0:T(8,128)(2,1)S(1)} collective-permute-done((bf16[1,64,2048]{2,1,0:T(8,128)(2,1)S(1)}, bf16[1,64,2048]{2,1,0:T(8,128)(2,1)S(1)}, u32[]{:S(2)}, u32[]{:S(2)}) %collective-permute-start.6) | collective-permute-done | bytes 262176 | tf_op jit(solution)/shard_map/ppermute | solution.py:13
  63.0 4.4 collective-permute-start.7
  67.4 8.8 %collective-permute-done.7 = bf16[1,128,2048]{2,1,0:T(8,128)(2,1)S(1)} collective-permute-done((bf16[1,128,2048]{2,1,0:T(8,128)(2,1)S(1)}, bf16[1,128,2048]{2,1,0:T(8,128)(2,1)S(1)}, u32[]{:S(2)}, u32[]{:S(2)}) %collective-permute-start.7) | collective-permute-done | bytes 524320 | tf_op jit(solution)/shard_map/ppermute | solution.py:13
  76.2 1.5 fusion.52
  77.7 5.5 collective-permute-start.8
  83.5 14.6 %collective-permute-done.8 = bf16[1,256,2048]{2,1,0:T(8,128)(2,1)} collective-permute-done((bf16[1,256,2048]{2,1,0:T(8,128)(2,1)}, bf16[1,256,2048]{2,1,0:T(8,128)(2,1)}, u32[]{:S(2)}, u32[]{:S(2)}) %collective-permute-start.8) | collective-permute-done | bytes 1048608 | tf_op jit(solution)/shard_map/ppermute | solution.py:13
  98.1 2.1 fusion.57
  100.2 17.4 %collective-permute-start.9 = (bf16[1,256,2048]{2,1,0:T(8,128)(2,1)S(1)}, bf16[1,256,2048]{2,1,0:T(8,128)(2,1)S(1)}, u32[]{:S(2)}, u32[]{:S(2)}) collective-permute-start(bf16[1,256,2048]{2,1,0:T(8,128)(2,1)S(1)} %fusion.57), channel_id=1, source_target_pairs={{0,8},{4,12},{1,9},{5,13},{2,10},{6,14},{3,11},{7,15},{16,24},{20,... | collective-permute-start | bytes 3145736 | tf_op jit(solution)/shard_map/ppermute | solution.py:13
  117.5 1.7 fusion.183
  119.4 10.2 %collective-permute-done.9 = bf16[1,256,2048]{2,1,0:T(8,128)(2,1)S(1)} collective-permute-done((bf16[1,256,2048]{2,1,0:T(8,128)(2,1)S(1)}, bf16[1,256,2048]{2,1,0:T(8,128)(2,1)S(1)}, u32[]{:S(2)}, u32[]{:S(2)}) %collective-permute-start.9) | collective-permute-done | bytes 1048608 | tf_op jit(solution)/shard_map/ppermute | solution.py:13
  130.9 13.8 %fusion.3 = (f32[1,256,2048]{2,1,0:T(8,128)}, bf16[1,256,2048]{2,1,0:T(8,128)(2,1)}) fusion(bf16[1,256,2048]{2,1,0:T(8,128)(2,1)S(1)} %fusion.57, bf16[1,256,2048]{2,1,0:T(8,128)(2,1)} %fusion.52, bf16[1,256,2048]{2,1,0:T(8,128)(2,1)} %copy-done.15, bf16[1,256,2048]{2,1,0:T(8,128)(2,1)} %copy-done.13, bf16[1,256,2048]{2,1,0:T(8,128)(2,1)S(1)} %copy-done.11, ...), kind=kLoop, calls=%fused_computation.123 | loop fusion | flops 70254592 | bytes 24275456 | tf_op jit(solution)/shard_map/add | solution.py:77
  144.8 11.1 %fusion.88 = (bf16[1,256,2048]{2,1,0:T(8,128)(2,1)S(1)}, f32[1,256,2048]{2,1,0:T(8,128)S(1)}) fusion(f32[2048]{0:T(1024)} %bitcast.180, f32[2048]{0:T(1024)S(1)} %bitcast.105, f32[2048]{0:T(1024)} %bitcast.133, pred[256]{0:T(512)(128)(4,1)} %get-tuple-element.139, f32[2048]{0:T(1024)} %bitcast.177, f32[2048]{0:T(1024)} %bitcast.186, f32[2048]{0:T(1024)} %bitcast.116, ...), kind=kOutput, calls=%fused_computation.208 | convolution fusion | flops 4315414528 | bytes 24183040 | tf_op jit(solution)/shard_map/bro,oc->brc/dot_general | solution.py:87
  155.9 1.3 collective-permute-start.10
  157.2 38.8 %collective-permute-done.10 = bf16[1,256,2048]{2,1,0:T(8,128)(2,1)S(1)} collective-permute-done((bf16[1,256,2048]{2,1,0:T(8,128)(2,1)S(1)}, bf16[1,256,2048]{2,1,0:T(8,128)(2,1)S(1)}, u32[]{:S(2)}, u32[]{:S(2)}) %collective-permute-start.10) | collective-permute-done | bytes 1048608 | tf_op jit(solution)/shard_map/ppermute | solution.py:13
  196.1 8.5 %fusion.4 = (f32[2048]{0:T(1024)}, f32[2048]{0:T(1024)}, f32[2048]{0:T(1024)}, f32[2048]{0:T(1024)}, f32[2048]{0:T(1024)}, /*index=5*/f32[2048]{0:T(1024)}, f32[...) fusion(f32[1,256,2048]{2,1,0:T(8,128)S(1)} %get-tuple-element.1, ...), kind=kLoop, calls=%fused_computation.124 | loop fusion | flops 47667200 | bytes 9691648 | tf_op jit(solution)/shard_map/reduce_sum | solution.py:100
  205.2 1.3 collective-permute-start.11
  206.5 21.0 %collective-permute-done.11 = bf16[1,256,2048]{2,1,0:T(8,128)(2,1)S(1)} collective-permute-done((bf16[1,256,2048]{2,1,0:T(8,128)(2,1)S(1)}, bf16[1,256,2048]{2,1,0:T(8,128)(2,1)S(1)}, u32[]{:S(2)}, u32[]{:S(2)}) %collective-permute-start.11) | collective-permute-done | bytes 1048608 | tf_op jit(solution)/shard_map/ppermute | solution.py:13
  227.5 1.5 fusion.105
  229.6 1.6 collective-permute-start.12
  231.3 12.4 %collective-permute-done.12 = bf16[1,128,2048]{2,1,0:T(8,128)(2,1)S(1)} collective-permute-done((bf16[1,128,2048]{2,1,0:T(8,128)(2,1)S(1)}, bf16[1,128,2048]{2,1,0:T(8,128)(2,1)S(1)}, u32[]{:S(2)}, u32[]{:S(2)}) %collective-permute-start.12) | collective-permute-done | bytes 524320 | tf_op jit(solution)/shard_map/ppermute | solution.py:13
  243.7 1.5 fusion.113
  245.2 4.6 multiply_reduce_fusion.2
  249.8 1.4 collective-permute-start.13
  251.3 6.9 %collective-permute-done.13 = bf16[1,64,2048]{2,1,0:T(8,128)(2,1)S(1)} collective-permute-done((bf16[1,64,2048]{2,1,0:T(8,128)(2,1)S(1)}, bf16[1,64,2048]{2,1,0:T(8,128)(2,1)S(1)}, u32[]{:S(2)}, u32[]{:S(2)}) %collective-permute-start.13) | collective-permute-done | bytes 262176 | tf_op jit(solution)/shard_map/ppermute | solution.py:13
  258.2 1.5 fusion.121
  263.0 12.5 %fusion.1 = bf16[1,256,4096]{2,1,0:T(8,128)(2,1)} fusion(bf16[4096,2048]{1,0:T(8,128)(2,1)} %param.12, f32[1,256,2048]{2,1,0:T(8,128)} %get-tuple-element.111), kind=kOutput, calls=%fused_computation.3 | convolution fusion | flops 4300734464 | bytes 20971520 | tf_op jit(solution)/shard_map/brc,oc->bro/dot_general | solution.py:79
  275.9 1.3 slice.165
  277.4 2.3 fusion.129
  279.8 3.8 multiply_reduce_fusion.4
  283.6 1.4 collective-permute-start.15
  285.1 5.4 collective-permute-done.15
  292.0 1.3 collective-permute-start.16
  293.4 4.4 collective-permute-done.16
  298.8 4.1 multiply_reduce_fusion.6
  302.9 1.4 collective-permute-start.17
  304.6 4.1 collective-permute-done.17
  310.3 1.6 collective-permute-start.18
  312.2 3.7 collective-permute-done.18
  316.0 2.0 fusion.161
  318.4 7.1 %multiply_reduce_fusion.8 = (f32[2048]{0:T(1024)}, f32[2048]{0:T(1024)}, f32[2048]{0:T(1024)}, f32[2048]{0:T(1024)}, f32[2048]{0:T(1024)}, /*index=5*/f32[2048]{...) fusion(f32[1,256,2048]{2,1,0:T(8,128)S(1)} %get-tuple-element.150, ...), kind=kLoop, calls=%fused_computation.295 | loop fusion | flops 25149440 | bytes 11641344 | tf_op jit(solution)/shard_map/reduce_sum | solution.py:111
  325.6 1.7 stack.67
  331.7 13.1 %fusion = bf16[4096,2048]{0,1:T(8,128)(2,1)} fusion(bf16[1,256,4096]{2,1,0:T(8,128)(2,1)} %all-gather.2.cloned.1.call-done, f32[1,256,2048]{2,1,0:T(8,128)} %get-tuple-element.111), kind=kOutput, calls=%fused_computation.1 | convolution fusion | flops 4316463104 | bytes 20971520 | tf_op jit(solution)/shard_map/bro,brc->oc/dot_general | solution.py:90
  346.0 1.3 collective-permute-start.19
  347.5 4.0 collective-permute-done.19
  351.6 1.7 add_convert_fusion
  353.3 28.3 %all-reduce.3.cloned.1.call-done = (bf16[2,2048]{1,0:T(2,128)(2,1)}, bf16[2,2048]{1,0:T(2,128)(2,1)}, bf16[13,2048]{1,0:T(8,128)(2,1)}) async-done(((bf16[2,2048]{1,0:T(2,128)(2,1)}, bf16[2,2048]{1,0:T(2,128)(2,1)}, bf16[13,2048]{1,0:T(8,128)(2,1)}), (bf16[2,2048]{1,0:T(2,128)(2,1)}, bf16[2,2048]{1,0:T(2,128)(2,1)}, bf16[13,2048]{1,0:T(8,128)(2,1)})) %all-reduce.3.cloned.1.call-update) | async-done | bytes 69648 | tf_op jit(solution)/shard_map/psum | solution.py:139
  381.6 1.3 convert_element_type.712
  382.9 1.3 convert_element_type.714
  384.2 1.5 convert_element_type.716
  385.7 169.5 %reduce-scatter.5.cloned.1.call-done = bf16[512,2048]{0,1:T(8,128)(2,1)} async-done(((bf16[4096,2048]{0,1:T(8,128)(2,1)}), bf16[512,2048]{0,1:T(8,128)(2,1)}) %reduce-scatter.5.cloned.1.call-update) | async-done | bytes 2097168 | tf_op jit(solution)/shard_map/reduce_scatter | solution.py:88
  555.2 3.9 copy.14
  (380 shorter events, 24.7 us)
Async XLA Ops:
  7.2 137.5 %all-gather.2.cloned.1.call-start = ((), (), s32[]{:S(2)}) async-start(), calls=%async_computation.3 | async-start | bytes 3145728 | tf_op jit(solution)/shard_map/all_gather | solution.py:86
  8.0 8.0 %collective-permute-start = (bf16[1,1,2048]{2,1,0:T(2,128)(2,1)S(1)}, bf16[1,1,2048]{2,1,0:T(2,128)(2,1)S(1)}, u32[]{:S(2)}, u32[]{:S(2)}) collective-permute-start(bf16[1,1,2048]{2,1,0:T(2,128)(2,1)S(1)} %slice.100), channel_id=1, source_target_pairs={{0,4},{4,8},{8,12},{1,5},{5,9},{9,13},{2,6},{6,10},{10,14},{3,7},{... | collective-permute-start | bytes 12296 | tf_op jit(solution)/shard_map/ppermute | solution.py:13
  15.9 26.8 %copy-start.143 = (pred[256]{0:T(512)(128)(4,1)}, pred[256]{0:T(512)(128)(4,1)S(1)}, u32[]{:S(2)}) copy-start(pred[256]{0:T(512)(128)(4,1)S(1)} %get-tuple-element.144) | copy-start | bytes 772
  16.0 35.3 %copy-start.129 = (pred[256]{0:T(512)(128)(4,1)}, pred[256]{0:T(512)(128)(4,1)S(1)}, u32[]{:S(2)}) copy-start(pred[256]{0:T(512)(128)(4,1)S(1)} %get-tuple-element.143) | copy-start | bytes 772
  16.0 46.3 %copy-start.146 = (pred[256]{0:T(512)(128)(4,1)}, pred[256]{0:T(512)(128)(4,1)S(1)}, u32[]{:S(2)}) copy-start(pred[256]{0:T(512)(128)(4,1)S(1)} %get-tuple-element.142) | copy-start | bytes 772
  16.0 60.2 %copy-start.133 = (pred[256]{0:T(512)(128)(4,1)}, pred[256]{0:T(512)(128)(4,1)S(1)}, u32[]{:S(2)}) copy-start(pred[256]{0:T(512)(128)(4,1)S(1)} %get-tuple-element.141) | copy-start | bytes 772
  18.3 111.4 %copy-start = (bf16[1,256,2048]{2,1,0:T(8,128)(2,1)}, bf16[1,256,2048]{2,1,0:T(8,128)(2,1)S(1)}, u32[]{:S(2)}) copy-start(bf16[1,256,2048]{2,1,0:T(8,128)(2,1)S(1)} %fusion.18) | copy-start | bytes 3145732
  18.3 4.8 collective-permute-start.1
  23.9 5.6 collective-permute-start.2
  30.2 5.8 %collective-permute-start.3 = (bf16[1,8,2048]{2,1,0:T(8,128)(2,1)S(1)}, bf16[1,8,2048]{2,1,0:T(8,128)(2,1)S(1)}, u32[]{:S(2)}, u32[]{:S(2)}) collective-permute-start(bf16[1,8,2048]{2,1,0:T(8,128)(2,1)S(1)} %slice.151), channel_id=1, source_target_pairs={{0,4},{4,8},{8,12},{1,5},{5,9},{9,13},{2,6},{6,10},{10,14},{3,7},{... | collective-permute-start | bytes 98312 | tf_op jit(solution)/shard_map/ppermute | solution.py:13
  36.7 6.1 %collective-permute-start.4 = (bf16[1,16,2048]{2,1,0:T(8,128)(2,1)S(1)}, bf16[1,16,2048]{2,1,0:T(8,128)(2,1)S(1)}, u32[]{:S(2)}, u32[]{:S(2)}) collective-permute-start(bf16[1,16,2048]{2,1,0:T(8,128)(2,1)S(1)} %slice.153), channel_id=1, source_target_pairs={{0,4},{4,8},{8,12},{1,5},{5,9},{9,13},{2,6},{6,10},{10,14},{3,7},{... | collective-permute-start | bytes 196616 | tf_op jit(solution)/shard_map/ppermute | solution.py:13
  43.4 7.8 %collective-permute-start.5 = (bf16[1,32,2048]{2,1,0:T(8,128)(2,1)S(1)}, bf16[1,32,2048]{2,1,0:T(8,128)(2,1)S(1)}, u32[]{:S(2)}, u32[]{:S(2)}) collective-permute-start(bf16[1,32,2048]{2,1,0:T(8,128)(2,1)S(1)} %slice.155), channel_id=1, source_target_pairs={{0,4},{4,8},{8,12},{1,5},{5,9},{9,13},{2,6},{6,10},{10,14},{3,7},{... | collective-permute-start | bytes 393224 | tf_op jit(solution)/shard_map/ppermute | solution.py:13
  51.8 10.5 %collective-permute-start.6 = (bf16[1,64,2048]{2,1,0:T(8,128)(2,1)S(1)}, bf16[1,64,2048]{2,1,0:T(8,128)(2,1)S(1)}, u32[]{:S(2)}, u32[]{:S(2)}) collective-permute-start(bf16[1,64,2048]{2,1,0:T(8,128)(2,1)S(1)} %slice.157), channel_id=1, source_target_pairs={{0,4},{4,8},{8,12},{1,5},{5,9},{9,13},{2,6},{6,10},{10,14},{3,7},{... | collective-permute-start | bytes 786440 | tf_op jit(solution)/shard_map/ppermute | solution.py:13
  63.0 13.2 %collective-permute-start.7 = (bf16[1,128,2048]{2,1,0:T(8,128)(2,1)S(1)}, bf16[1,128,2048]{2,1,0:T(8,128)(2,1)S(1)}, u32[]{:S(2)}, u32[]{:S(2)}) collective-permute-start(bf16[1,128,2048]{2,1,0:T(8,128)(2,1)S(1)} %get-tuple-element.120), channel_id=1, source_target_pairs={{0,4},{4,8},{8,12},{1,5},{5,9},{9,13},{2,6},{6,10},{10,14},{3,7},{... | collective-permute-start | bytes 1572872 | tf_op jit(solution)/shard_map/ppermute | solution.py:13
  77.7 53.0 %copy-start.2 = (bf16[1,256,2048]{2,1,0:T(8,128)(2,1)S(1)}, bf16[1,256,2048]{2,1,0:T(8,128)(2,1)}, u32[]{:S(2)}) copy-start(bf16[1,256,2048]{2,1,0:T(8,128)(2,1)} %param.7) | copy-start | bytes 3145732
  77.7 20.4 %collective-permute-start.8 = (bf16[1,256,2048]{2,1,0:T(8,128)(2,1)}, bf16[1,256,2048]{2,1,0:T(8,128)(2,1)}, u32[]{:S(2)}, u32[]{:S(2)}) collective-permute-start(bf16[1,256,2048]{2,1,0:T(8,128)(2,1)} %fusion.52), channel_id=1, source_target_pairs={{0,4},{4,8},{8,12},{1,5},{5,9},{9,13},{2,6},{6,10},{10,14},{3,7},{... | collective-permute-start | bytes 3145736 | tf_op jit(solution)/shard_map/ppermute | solution.py:13
  83.2 234.9 %reduce-scatter.3.cloned.1.call-start = ((), (), s32[]{:S(2)}) async-start(), calls=%async_computation.2 | async-start | bytes 3145728 | tf_op jit(solution)/shard_map/reduce_scatter | solution.py:82
  83.3 35.9 %copy-start.139 = (f32[2,2048]{1,0:T(2,128)S(1)}, f32[2,2048]{1,0:T(2,128)}, u32[]{:S(2)}) copy-start(f32[2,2048]{1,0:T(2,128)} %param.10) | copy-start | bytes 49156
  83.3 47.4 %copy-start.5 = (bf16[1,256,2048]{2,1,0:T(8,128)(2,1)S(1)}, bf16[1,256,2048]{2,1,0:T(8,128)(2,1)}, u32[]{:S(2)}) copy-start(bf16[1,256,2048]{2,1,0:T(8,128)(2,1)} %copy-done.4) | copy-start | bytes 3145732
  83.3 47.4 %copy-start.8 = (bf16[1,256,2048]{2,1,0:T(8,128)(2,1)S(1)}, bf16[1,256,2048]{2,1,0:T(8,128)(2,1)}, u32[]{:S(2)}) copy-start(bf16[1,256,2048]{2,1,0:T(8,128)(2,1)} %copy-done.7) | copy-start | bytes 3145732
  83.3 47.4 %copy-start.11 = (bf16[1,256,2048]{2,1,0:T(8,128)(2,1)S(1)}, bf16[1,256,2048]{2,1,0:T(8,128)(2,1)}, u32[]{:S(2)}) copy-start(bf16[1,256,2048]{2,1,0:T(8,128)(2,1)} %copy-done.10) | copy-start | bytes 3145732
  83.3 47.4 %copy-start.49 = (bf16[1,16,2048]{2,1,0:T(8,128)(2,1)S(1)}, bf16[1,16,2048]{2,1,0:T(8,128)(2,1)}, u32[]{:S(2)}) copy-start(bf16[1,16,2048]{2,1,0:T(8,128)(2,1)} %copy-done.48) | copy-start | bytes 196612
  83.3 47.4 %copy-start.52 = (bf16[1,8,2048]{2,1,0:T(8,128)(2,1)S(1)}, bf16[1,8,2048]{2,1,0:T(8,128)(2,1)}, u32[]{:S(2)}) copy-start(bf16[1,8,2048]{2,1,0:T(8,128)(2,1)} %copy-done.51) | copy-start | bytes 98308
  83.4 47.4 %copy-start.55 = (bf16[1,4,2048]{2,1,0:T(4,128)(2,1)S(1)}, bf16[1,4,2048]{2,1,0:T(4,128)(2,1)}, u32[]{:S(2)}) copy-start(bf16[1,4,2048]{2,1,0:T(4,128)(2,1)} %copy-done.54) | copy-start | bytes 49156
  83.4 47.4 %copy-start.69 = (bf16[1,1,2048]{2,1,0:T(2,128)(2,1)S(1)}, bf16[1,1,2048]{2,1,0:T(2,128)(2,1)}, u32[]{:S(2)}) copy-start(bf16[1,1,2048]{2,1,0:T(2,128)(2,1)} %copy-done.68) | copy-start | bytes 12292
  83.4 47.4 %copy-start.72 = (bf16[1,2,2048]{2,1,0:T(2,128)(2,1)S(1)}, bf16[1,2,2048]{2,1,0:T(2,128)(2,1)}, u32[]{:S(2)}) copy-start(bf16[1,2,2048]{2,1,0:T(2,128)(2,1)} %copy-done.71) | copy-start | bytes 24580
  83.4 47.4 %copy-start.127 = (pred[256]{0:T(512)(128)(4,1)S(1)}, pred[256]{0:T(512)(128)(4,1)}, u32[]{:S(2)}) copy-start(pred[256]{0:T(512)(128)(4,1)} %copy-done.126) | copy-start | bytes 772
  83.4 47.4 %copy-start.130 = (pred[256]{0:T(512)(128)(4,1)S(1)}, pred[256]{0:T(512)(128)(4,1)}, u32[]{:S(2)}) copy-start(pred[256]{0:T(512)(128)(4,1)} %copy-done.129) | copy-start | bytes 772
  83.4 47.4 %copy-start.134 = (pred[256]{0:T(512)(128)(4,1)S(1)}, pred[256]{0:T(512)(128)(4,1)}, u32[]{:S(2)}) copy-start(pred[256]{0:T(512)(128)(4,1)} %copy-done.133) | copy-start | bytes 772
  83.4 47.4 %copy-start.137 = (pred[256]{0:T(512)(128)(4,1)S(1)}, pred[256]{0:T(512)(128)(4,1)}, u32[]{:S(2)}) copy-start(pred[256]{0:T(512)(128)(4,1)} %copy-done.136) | copy-start | bytes 772
  83.4 47.4 %copy-start.141 = (pred[256]{0:T(512)(128)(4,1)S(1)}, pred[256]{0:T(512)(128)(4,1)}, u32[]{:S(2)}) copy-start(pred[256]{0:T(512)(128)(4,1)} %copy-done.140) | copy-start | bytes 772
  83.4 47.4 %copy-start.144 = (pred[256]{0:T(512)(128)(4,1)S(1)}, pred[256]{0:T(512)(128)(4,1)}, u32[]{:S(2)}) copy-start(pred[256]{0:T(512)(128)(4,1)} %copy-done.143) | copy-start | bytes 772
  83.4 47.4 %copy-start.147 = (pred[256]{0:T(512)(128)(4,1)S(1)}, pred[256]{0:T(512)(128)(4,1)}, u32[]{:S(2)}) copy-start(pred[256]{0:T(512)(128)(4,1)} %copy-done.146) | copy-start | bytes 772
  83.5 47.4 %copy-start.149 = (pred[256]{0:T(512)(128)(4,1)S(1)}, pred[256]{0:T(512)(128)(4,1)}, u32[]{:S(2)}) copy-start(pred[256]{0:T(512)(128)(4,1)} %get-tuple-element.140) | copy-start | bytes 772
  83.5 47.4 %copy-start.152 = (pred[256]{0:T(512)(128)(4,1)S(1)}, pred[256]{0:T(512)(128)(4,1)}, u32[]{:S(2)}) copy-start(pred[256]{0:T(512)(128)(4,1)} %copy-done.151) | copy-start | bytes 772
  83.5 47.4 %copy-start.154 = (pred[256]{0:T(512)(128)(4,1)S(1)}, pred[256]{0:T(512)(128)(4,1)}, u32[]{:S(2)}) copy-start(pred[256]{0:T(512)(128)(4,1)} %get-tuple-element.139) | copy-start | bytes 772
  100.2 29.5 %copy-start.31 = (bf16[1,256,2048]{2,1,0:T(8,128)(2,1)}, bf16[1,256,2048]{2,1,0:T(8,128)(2,1)S(1)}, u32[]{:S(2)}) copy-start(bf16[1,256,2048]{2,1,0:T(8,128)(2,1)S(1)} %fusion.57) | copy-start | bytes 3145732
  100.2 29.5 %collective-permute-start.9 = (bf16[1,256,2048]{2,1,0:T(8,128)(2,1)S(1)}, bf16[1,256,2048]{2,1,0:T(8,128)(2,1)S(1)}, u32[]{:S(2)}, u32[]{:S(2)}) collective-permute-start(bf16[1,256,2048]{2,1,0:T(8,128)(2,1)S(1)} %fusion.57), channel_id=1, source_target_pairs={{0,8},{4,12},{1,9},{5,13},{2,10},{6,14},{3,11},{7,15},{16,24},{20,... | collective-permute-start | bytes 3145736 | tf_op jit(solution)/shard_map/ppermute | solution.py:13
  144.6 51.4 %copy-start.32 = (bf16[1,256,2048]{2,1,0:T(8,128)(2,1)S(1)}, bf16[1,256,2048]{2,1,0:T(8,128)(2,1)}, u32[]{:S(2)}) copy-start(bf16[1,256,2048]{2,1,0:T(8,128)(2,1)} %copy-done.31) | copy-start | bytes 3145732
  144.7 51.4 %copy-start.38 = (bf16[1,256,2048]{2,1,0:T(8,128)(2,1)S(1)}, bf16[1,256,2048]{2,1,0:T(8,128)(2,1)}, u32[]{:S(2)}) copy-start(bf16[1,256,2048]{2,1,0:T(8,128)(2,1)} %copy-done.37) | copy-start | bytes 3145732
  144.7 51.4 %copy-start.39 = (bf16[1,256,2048]{2,1,0:T(8,128)(2,1)S(1)}, bf16[1,256,2048]{2,1,0:T(8,128)(2,1)}, u32[]{:S(2)}) copy-start(bf16[1,256,2048]{2,1,0:T(8,128)(2,1)} %get-tuple-element.112) | copy-start | bytes 3145732
  144.7 51.3 %copy-start.43 = (f32[1,2048]{1,0:T(1,128)S(1)}, f32[1,2048]{1,0:T(1,128)}, u32[]{:S(2)}) copy-start(f32[1,2048]{1,0:T(1,128)} %copy-done.42) | copy-start | bytes 24580
  144.7 51.3 %copy-start.46 = (f32[1,2048]{1,0:T(1,128)S(1)}, f32[1,2048]{1,0:T(1,128)}, u32[]{:S(2)}) copy-start(f32[1,2048]{1,0:T(1,128)} %copy-done.45) | copy-start | bytes 24580
  144.7 51.3 %copy-start.67 = (f32[1,2048]{1,0:T(1,128)S(1)}, f32[1,2048]{1,0:T(1,128)}, u32[]{:S(2)}) copy-start(f32[1,2048]{1,0:T(1,128)} %copy-done.66) | copy-start | bytes 24580
  144.7 51.3 %copy-start.83 = (f32[2048]{0:T(1024)S(1)}, f32[2048]{0:T(1024)}, u32[]{:S(2)}) copy-start(f32[2048]{0:T(1024)} %copy-done.82) | copy-start | bytes 24580
  144.7 51.3 %copy-start.85 = (f32[2048]{0:T(1024)S(1)}, f32[2048]{0:T(1024)}, u32[]{:S(2)}) copy-start(f32[2048]{0:T(1024)} %copy-done.84) | copy-start | bytes 24580
  144.7 51.3 %copy-start.87 = (f32[1,2048]{1,0:T(1,128)S(1)}, f32[1,2048]{1,0:T(1,128)}, u32[]{:S(2)}) copy-start(f32[1,2048]{1,0:T(1,128)} %copy-done.86) | copy-start | bytes 24580
  144.7 51.3 %copy-start.89 = (f32[1,2048]{1,0:T(1,128)S(1)}, f32[1,2048]{1,0:T(1,128)}, u32[]{:S(2)}) copy-start(f32[1,2048]{1,0:T(1,128)} %copy-done.88) | copy-start | bytes 24580
  144.8 51.3 %copy-start.91 = (f32[1,2048]{1,0:T(1,128)S(1)}, f32[1,2048]{1,0:T(1,128)}, u32[]{:S(2)}) copy-start(f32[1,2048]{1,0:T(1,128)} %copy-done.90) | copy-start | bytes 24580
  144.8 51.3 %copy-start.93 = (f32[1,2048]{1,0:T(1,128)S(1)}, f32[1,2048]{1,0:T(1,128)}, u32[]{:S(2)}) copy-start(f32[1,2048]{1,0:T(1,128)} %copy-done.92) | copy-start | bytes 24580
  144.8 51.3 %copy-start.150 = (pred[256]{0:T(512)(128)(4,1)S(1)}, pred[256]{0:T(512)(128)(4,1)}, u32[]{:S(2)}) copy-start(pred[256]{0:T(512)(128)(4,1)} %get-tuple-element.140) | copy-start | bytes 772
  144.8 51.3 %copy-start.155 = (pred[256]{0:T(512)(128)(4,1)S(1)}, pred[256]{0:T(512)(128)(4,1)}, u32[]{:S(2)}) copy-start(pred[256]{0:T(512)(128)(4,1)} %get-tuple-element.139) | copy-start | bytes 772
  155.9 40.1 %collective-permute-start.10 = (bf16[1,256,2048]{2,1,0:T(8,128)(2,1)S(1)}, bf16[1,256,2048]{2,1,0:T(8,128)(2,1)S(1)}, u32[]{:S(2)}, u32[]{:S(2)}) collective-permute-start(bf16[1,256,2048]{2,1,0:T(8,128)(2,1)S(1)} %get-tuple-element.149), channel_id=1, source_target_pairs={{8,0},{12,4},{9,1},{13,5},{10,2},{14,6},{11,3},{15,7},{24,16},{28,... | collective-permute-start | bytes 3145736 | tf_op jit(solution)/shard_map/ppermute | solution.py:13
  205.2 22.3 %collective-permute-start.11 = (bf16[1,256,2048]{2,1,0:T(8,128)(2,1)S(1)}, bf16[1,256,2048]{2,1,0:T(8,128)(2,1)S(1)}, u32[]{:S(2)}, u32[]{:S(2)}) collective-permute-start(bf16[1,256,2048]{2,1,0:T(8,128)(2,1)S(1)} %fusion.96), channel_id=1, source_target_pairs={{4,0},{8,4},{12,8},{5,1},{9,5},{13,9},{6,2},{10,6},{14,10},{7,3},{... | collective-permute-start | bytes 3145736 | tf_op jit(solution)/shard_map/ppermute | solution.py:13
  229.6 14.0 %collective-permute-start.12 = (bf16[1,128,2048]{2,1,0:T(8,128)(2,1)S(1)}, bf16[1,128,2048]{2,1,0:T(8,128)(2,1)S(1)}, u32[]{:S(2)}, u32[]{:S(2)}) collective-permute-start(bf16[1,128,2048]{2,1,0:T(8,128)(2,1)S(1)} %get-tuple-element.119), channel_id=1, source_target_pairs={{4,0},{8,4},{12,8},{5,1},{9,5},{13,9},{6,2},{10,6},{14,10},{7,3},{... | collective-permute-start | bytes 1572872 | tf_op jit(solution)/shard_map/ppermute | solution.py:13
  249.8 8.4 %collective-permute-start.13 = (bf16[1,64,2048]{2,1,0:T(8,128)(2,1)S(1)}, bf16[1,64,2048]{2,1,0:T(8,128)(2,1)S(1)}, u32[]{:S(2)}, u32[]{:S(2)}) collective-permute-start(bf16[1,64,2048]{2,1,0:T(8,128)(2,1)S(1)} %slice.164), channel_id=1, source_target_pairs={{4,0},{8,4},{12,8},{5,1},{9,5},{13,9},{6,2},{10,6},{14,10},{7,3},{... | collective-permute-start | bytes 786440 | tf_op jit(solution)/shard_map/ppermute | solution.py:13
  261.7 15.7 %collective-permute-start.14 = (bf16[1,32,2048]{2,1,0:T(8,128)(2,1)}, bf16[1,32,2048]{2,1,0:T(8,128)(2,1)S(1)}, u32[]{:S(2)}, u32[]{:S(2)}) collective-permute-start(bf16[1,32,2048]{2,1,0:T(8,128)(2,1)} %slice.166), channel_id=1, source_target_pairs={{4,0},{8,4},{12,8},{5,1},{9,5},{13,9},{6,2},{10,6},{14,10},{7,3},{... | collective-permute-start | bytes 393224 | tf_op jit(solution)/shard_map/ppermute | solution.py:13
  275.5 106.1 %all-reduce.3.cloned.1.call-start = ((), (), s32[]{:S(2)}) async-start(), calls=%async_computation.5 | async-start | bytes 163840 | tf_op jit(solution)/shard_map/psum | solution.py:139
  283.6 6.9 %collective-permute-start.15 = (bf16[1,16,2048]{2,1,0:T(8,128)(2,1)S(1)}, bf16[1,16,2048]{2,1,0:T(8,128)(2,1)S(1)}, u32[]{:S(2)}, u32[]{:S(2)}) collective-permute-start(bf16[1,16,2048]{2,1,0:T(8,128)(2,1)S(1)} %slice.168), channel_id=1, source_target_pairs={{4,0},{8,4},{12,8},{5,1},{9,5},{13,9},{6,2},{10,6},{14,10},{7,3},{... | collective-permute-start | bytes 196616 | tf_op jit(solution)/shard_map/ppermute | solution.py:13
  292.0 5.8 %collective-permute-start.16 = (bf16[1,8,2048]{2,1,0:T(8,128)(2,1)S(1)}, bf16[1,8,2048]{2,1,0:T(8,128)(2,1)S(1)}, u32[]{:S(2)}, u32[]{:S(2)}) collective-permute-start(bf16[1,8,2048]{2,1,0:T(8,128)(2,1)S(1)} %slice.170), channel_id=1, source_target_pairs={{4,0},{8,4},{12,8},{5,1},{9,5},{13,9},{6,2},{10,6},{14,10},{7,3},{... | collective-permute-start | bytes 98312 | tf_op jit(solution)/shard_map/ppermute | solution.py:13
  302.9 5.8 %collective-permute-start.17 = (bf16[1,4,2048]{2,1,0:T(4,128)(2,1)S(1)}, bf16[1,4,2048]{2,1,0:T(4,128)(2,1)S(1)}, u32[]{:S(2)}, u32[]{:S(2)}) collective-permute-start(bf16[1,4,2048]{2,1,0:T(4,128)(2,1)S(1)} %slice.172), channel_id=1, source_target_pairs={{4,0},{8,4},{12,8},{5,1},{9,5},{13,9},{6,2},{10,6},{14,10},{7,3},{... | collective-permute-start | bytes 49160 | tf_op jit(solution)/shard_map/ppermute | solution.py:13
  310.3 5.7 %collective-permute-start.18 = (bf16[1,2,2048]{2,1,0:T(2,128)(2,1)S(1)}, bf16[1,2,2048]{2,1,0:T(2,128)(2,1)S(1)}, u32[]{:S(2)}, u32[]{:S(2)}) collective-permute-start(bf16[1,2,2048]{2,1,0:T(2,128)(2,1)S(1)} %slice.348), channel_id=1, source_target_pairs={{4,0},{8,4},{12,8},{5,1},{9,5},{13,9},{6,2},{10,6},{14,10},{7,3},{... | collective-permute-start | bytes 24584 | tf_op jit(solution)/shard_map/ppermute | solution.py:13
  331.6 223.6 %reduce-scatter.5.cloned.1.call-start = ((), (), s32[]{:S(2)}) async-start(), calls=%async_computation.4 | async-start | bytes 18874368 | tf_op jit(solution)/shard_map/reduce_scatter | solution.py:88
  346.0 5.6 collective-permute-start.19
  (116 other events, 937.8 us)
Sparse Core Ops, SparseCore 0:
  83.4 32.4 all-gather.1
  275.6 32.0 reduce-scatter.2
  331.7 49.8 all-reduce.2
  383.8 171.3 reduce-scatter.4
where the time goes:
time: 573 us; the launch traced here: 566 us
  waiting for transfers between devices  348 us (61%)
  other arithmetic  77.7 us (14%)
  starting transfers between devices  71.5 us (12%)
  matrix products  36.7 us (6%)
  between operations  16.3 us (3%)
  local copies, waits for them, and re-layouts  16.1 us (3%)
    reduce_scatter x1, waiting for transfers between devices, shards(): lax.psum_scatter((jnp.einsum('bro,brc->oc', gathered, activated, preferre...  170 us
    ppermute x20, waiting for transfers between devices, shifted_2(): return lax.ppermute(block, axis, route)  150 us
    ppermute x20, starting transfers between devices, shifted_2(): return lax.ppermute(block, axis, route)  70.9 us
    psum x1, waiting for transfers between devices, shards(): lax.psum(low_grad.astype(jnp.bfloat16), ('seq', 'dp')).astype(jnp.float32)  28.3 us
    reduce_sum x4, other arithmetic, shards(): weight_sums[level_index] = jnp.sum(summed_grad * highpass, axis=(0, 1))  19.5 us
    add x1, other arithmetic, shards(): summed = summed + level_weights[levels] * current  13.8 us
    dot_general x1, matrix products, shards(): jnp.einsum('bro,brc->oc', gathered, activated, preferred_element_type=jnp...  13.1 us
    dot_general x1, matrix products, shards(): jnp.einsum('brc,oc->bro', activated, mix_weight, preferred_element_type=j...  12.5 us
  transfers between devices with their start and end apart: 24, of which 20 were waited for; matrix products, arithmetic and copies ran while one was open for 12% of the time, Pallas kernels for 0%

commit v1 on v0

--- a/solution.py
+++ b/solution.py
@@ -136,7 +136,9 @@
     high_grad = jnp.stack([high_first, high_second]) * grad_scale
     level_grad = jnp.stack(weight_sums) * grad_scale
     low_grad, high_grad, level_grad = (
-        lax.psum(low_grad.astype(jnp.bfloat16), ("seq", "dp")).astype(jnp.float32),
+        jnp.sum(lax.all_gather(low_grad.astype(jnp.bfloat16), ("seq", "dp")), axis=0).astype(
+            jnp.float32
+        ),
         lax.psum(high_grad.astype(jnp.bfloat16), ("seq", "dp")).astype(jnp.float32),
         lax.psum(level_grad.astype(jnp.bfloat16), ("seq", "dp")).astype(jnp.float32),
     )

time: 573 us -> 483 us (0.84)
  waiting for transfers between devices: 348 us -> 221 us
  blocking collectives: 0 us -> 43.3 us
  other arithmetic: 77.7 us -> 71.9 us
    reduce_scatter x1, waiting for transfers between devices: 170 us -> 0.01 us  [shards(): lax.psum_scatter((jnp.einsum('bro,brc->oc', gathered, activated, preferre...]
    ppermute x20, waiting for transfers between devices: 150 us -> 221 us  [shifted_2(): return lax.ppermute(block, axis, route)]
    psum x0 -> x1, blocking collectives: none -> 29.3 us  [shards(): lax.psum(high_grad.astype(jnp.bfloat16), ('seq', 'dp')).astype(jnp.float32)]
    psum x1 -> x0, waiting for transfers between devices: 28.3 us -> none  [shards(): lax.psum(low_grad.astype(jnp.bfloat16), ('seq', 'dp')).astype(jnp.float32)]
    all_gather x0 -> x1, blocking collectives: none -> 14 us  [shards(): lax.all_gather(low_grad.astype(jnp.bfloat16), ('seq', 'dp'))]
  transfers between devices with their start and end apart: 24 -> 23, of which waited for: 20 -> 18; matrix products, arithmetic and copies ran while one was open for 12% -> 23% of each run, Pallas kernels for 0% -> 0%
where the time goes in v1:
time: 483 us; the launch traced here: 476 us
  waiting for transfers between devices  221 us (46%)
  other arithmetic  71.9 us (15%)
  starting transfers between devices  71.8 us (15%)
  blocking collectives  43.3 us (9%)
  matrix products  33.6 us (7%)
  local copies, waits for them, and re-layouts  17.6 us (4%)
  between operations  16.5 us (3%)
    ppermute x20, waiting for transfers between devices, shifted_2(): return lax.ppermute(block, axis, route)  221 us
    ppermute x20, starting transfers between devices, shifted_2(): return lax.ppermute(block, axis, route)  71.5 us
    psum x1, blocking collectives, shards(): lax.psum(high_grad.astype(jnp.bfloat16), ('seq', 'dp')).astype(jnp.float32)  29.3 us
    reduce_sum x4, other arithmetic, shards(): weight_sums[level_index] = jnp.sum(summed_grad * highpass, axis=(0, 1))  19.4 us
    all_gather x1, blocking collectives, shards(): lax.all_gather(low_grad.astype(jnp.bfloat16), ('seq', 'dp'))  14 us
    add x1, other arithmetic, shards(): summed = summed + level_weights[levels] * current  13.8 us
    dot_general x1, matrix products, shards(): jnp.einsum('brc,oc->bro', activated, mix_weight, preferred_element_type=j...  12.4 us
    dot_general x1, matrix products, shards(): jnp.einsum('bro,oc->brc', gathered, mix_weight, preferred_element_type=jn...  11.1 us
  transfers between devices with their start and end apart: 23, of which 18 were waited for; matrix products, arithmetic and copies ran while one was open for 23% of the time, Pallas kernels for 0%

profile of v1, /device:TPU:0, one launch (start us, length us, event | category | flops | bytes accessed | tf_op | source)
XLA Modules:
  0.0 475.9 jit_solution(15013602706500502552)
XLA Ops:
  8.0 4.9 %collective-permute-start = (bf16[1,1,2048]{2,1,0:T(2,128)(2,1)S(1)}, bf16[1,1,2048]{2,1,0:T(2,128)(2,1)S(1)}, u32[]{:S(2)}, u32[]{:S(2)}) collective-permute-start(bf16[1,1,2048]{2,1,0:T(2,128)(2,1)S(1)} %slice.100), channel_id=1, source_target_pairs={{0,4},{4,8},{8,12},{1,5},{5,9},{9,13},{2,6},{6,10},{10,14},{3,7},{... | collective-permute-start | bytes 12296 | tf_op jit(solution)/shard_map/ppermute | solution.py:13
  16.0 2.3 fusion.18
  18.3 3.5 collective-permute-start.1
  21.8 1.3 collective-permute-done.1
  23.9 4.2 collective-permute-start.2
  28.1 1.4 collective-permute-done.2
  30.3 4.2 collective-permute-start.3
  34.6 1.5 collective-permute-done.3
  36.7 4.2 collective-permute-start.4
  41.0 1.8 collective-permute-done.4
  43.4 4.3 collective-permute-start.5
  47.8 3.5 collective-permute-done.5
  51.8 4.4 collective-permute-start.6
  56.3 6.0 %collective-permute-done.6 = bf16[1,64,2048]{2,1,0:T(8,128)(2,1)S(1)} collective-permute-done((bf16[1,64,2048]{2,1,0:T(8,128)(2,1)S(1)}, bf16[1,64,2048]{2,1,0:T(8,128)(2,1)S(1)}, u32[]{:S(2)}, u32[]{:S(2)}) %collective-permute-start.6) | collective-permute-done | bytes 262176 | tf_op jit(solution)/shard_map/ppermute | solution.py:13
  63.0 4.4 collective-permute-start.7
  67.4 8.8 %collective-permute-done.7 = bf16[1,128,2048]{2,1,0:T(8,128)(2,1)S(1)} collective-permute-done((bf16[1,128,2048]{2,1,0:T(8,128)(2,1)S(1)}, bf16[1,128,2048]{2,1,0:T(8,128)(2,1)S(1)}, u32[]{:S(2)}, u32[]{:S(2)}) %collective-permute-start.7) | collective-permute-done | bytes 524320 | tf_op jit(solution)/shard_map/ppermute | solution.py:13
  76.2 1.5 fusion.52
  77.7 5.6 %collective-permute-start.8 = (bf16[1,256,2048]{2,1,0:T(8,128)(2,1)}, bf16[1,256,2048]{2,1,0:T(8,128)(2,1)}, u32[]{:S(2)}, u32[]{:S(2)}) collective-permute-start(bf16[1,256,2048]{2,1,0:T(8,128)(2,1)} %fusion.52), channel_id=1, source_target_pairs={{0,4},{4,8},{8,12},{1,5},{5,9},{9,13},{2,6},{6,10},{10,14},{3,7},{... | collective-permute-start | bytes 3145736 | tf_op jit(solution)/shard_map/ppermute | solution.py:13
  83.5 14.5 %collective-permute-done.8 = bf16[1,256,2048]{2,1,0:T(8,128)(2,1)} collective-permute-done((bf16[1,256,2048]{2,1,0:T(8,128)(2,1)}, bf16[1,256,2048]{2,1,0:T(8,128)(2,1)}, u32[]{:S(2)}, u32[]{:S(2)}) %collective-permute-start.8) | collective-permute-done | bytes 1048608 | tf_op jit(solution)/shard_map/ppermute | solution.py:13
  98.1 2.1 fusion.57
  100.2 17.7 %collective-permute-start.9 = (bf16[1,256,2048]{2,1,0:T(8,128)(2,1)S(1)}, bf16[1,256,2048]{2,1,0:T(8,128)(2,1)S(1)}, u32[]{:S(2)}, u32[]{:S(2)}) collective-permute-start(bf16[1,256,2048]{2,1,0:T(8,128)(2,1)S(1)} %fusion.57), channel_id=1, source_target_pairs={{0,8},{4,12},{1,9},{5,13},{2,10},{6,14},{3,11},{7,15},{16,24},{20,... | collective-permute-start | bytes 3145736 | tf_op jit(solution)/shard_map/ppermute | solution.py:13
  118.7 1.7 fusion.183
  120.6 9.1 %collective-permute-done.9 = bf16[1,256,2048]{2,1,0:T(8,128)(2,1)S(1)} collective-permute-done((bf16[1,256,2048]{2,1,0:T(8,128)(2,1)S(1)}, bf16[1,256,2048]{2,1,0:T(8,128)(2,1)S(1)}, u32[]{:S(2)}, u32[]{:S(2)}) %collective-permute-start.9) | collective-permute-done | bytes 1048608 | tf_op jit(solution)/shard_map/ppermute | solution.py:13
  129.9 13.8 %fusion.3 = (f32[1,256,2048]{2,1,0:T(8,128)}, bf16[1,256,2048]{2,1,0:T(8,128)(2,1)}) fusion(bf16[1,256,2048]{2,1,0:T(8,128)(2,1)S(1)} %fusion.57, bf16[1,256,2048]{2,1,0:T(8,128)(2,1)} %fusion.52, bf16[1,256,2048]{2,1,0:T(8,128)(2,1)} %copy-done.15, bf16[1,256,2048]{2,1,0:T(8,128)(2,1)} %copy-done.13, bf16[1,256,2048]{2,1,0:T(8,128)(2,1)S(1)} %copy-done.11, ...), kind=kLoop, calls=%fused_computation.123 | loop fusion | flops 70254592 | bytes 24275456 | tf_op jit(solution)/shard_map/add | solution.py:77
  143.8 12.4 %fusion.1 = bf16[1,256,4096]{2,1,0:T(8,128)(2,1)} fusion(bf16[4096,2048]{1,0:T(8,128)(2,1)} %param.12, f32[1,256,2048]{2,1,0:T(8,128)} %get-tuple-element.116), kind=kOutput, calls=%fused_computation.3 | convolution fusion | flops 4300734464 | bytes 20971520 | tf_op jit(solution)/shard_map/brc,oc->bro/dot_general | solution.py:79
  156.5 1.3 copy-done.37
  157.9 10.0 %fusion = bf16[4096,2048]{0,1:T(8,128)(2,1)} fusion(bf16[1,256,4096]{2,1,0:T(8,128)(2,1)} %all-gather.2.cloned.1.call-done, f32[1,256,2048]{2,1,0:T(8,128)S(1)} %copy-done.37), kind=kOutput, calls=%fused_computation.1 | convolution fusion | flops 4316463104 | bytes 20971520 | tf_op jit(solution)/shard_map/bro,brc->oc/dot_general | solution.py:90
  168.1 11.1 %fusion.88 = (bf16[1,256,2048]{2,1,0:T(8,128)(2,1)S(1)}, f32[1,256,2048]{2,1,0:T(8,128)S(1)}) fusion(f32[2048]{0:T(1024)} %bitcast.180, f32[2048]{0:T(1024)S(1)} %bitcast.105, f32[2048]{0:T(1024)} %bitcast.133, pred[256]{0:T(512)(128)(4,1)} %get-tuple-element.144, f32[2048]{0:T(1024)} %bitcast.177, f32[2048]{0:T(1024)} %bitcast.186, f32[2048]{0:T(1024)} %bitcast.116, ...), kind=kOutput, calls=%fused_computation.208 | convolution fusion | flops 4315414528 | bytes 24183040 | tf_op jit(solution)/shard_map/bro,oc->brc/dot_general | solution.py:87
  179.2 1.3 collective-permute-start.10
  180.5 54.0 %collective-permute-done.10 = bf16[1,256,2048]{2,1,0:T(8,128)(2,1)S(1)} collective-permute-done((bf16[1,256,2048]{2,1,0:T(8,128)(2,1)S(1)}, bf16[1,256,2048]{2,1,0:T(8,128)(2,1)S(1)}, u32[]{:S(2)}, u32[]{:S(2)}) %collective-permute-start.10) | collective-permute-done | bytes 1048608 | tf_op jit(solution)/shard_map/ppermute | solution.py:13
  234.6 8.5 %fusion.4 = (f32[2048]{0:T(1024)}, f32[2048]{0:T(1024)}, f32[2048]{0:T(1024)}, f32[2048]{0:T(1024)}, f32[2048]{0:T(1024)}, /*index=5*/f32[2048]{0:T(1024)}, f32[...) fusion(f32[1,256,2048]{2,1,0:T(8,128)S(1)} %get-tuple-element.1, ...), kind=kLoop, calls=%fused_computation.124 | loop fusion | flops 47667200 | bytes 9691648 | tf_op jit(solution)/shard_map/reduce_sum | solution.py:100
  243.6 1.3 collective-permute-start.11
  244.9 49.0 %collective-permute-done.11 = bf16[1,256,2048]{2,1,0:T(8,128)(2,1)S(1)} collective-permute-done((bf16[1,256,2048]{2,1,0:T(8,128)(2,1)S(1)}, bf16[1,256,2048]{2,1,0:T(8,128)(2,1)S(1)}, u32[]{:S(2)}, u32[]{:S(2)}) %collective-permute-start.11) | collective-permute-done | bytes 1048608 | tf_op jit(solution)/shard_map/ppermute | solution.py:13
  294.0 0.9 fusion.105
  295.5 1.6 collective-permute-start.12
  297.1 25.1 %collective-permute-done.12 = bf16[1,128,2048]{2,1,0:T(8,128)(2,1)S(1)} collective-permute-done((bf16[1,128,2048]{2,1,0:T(8,128)(2,1)S(1)}, bf16[1,128,2048]{2,1,0:T(8,128)(2,1)S(1)}, u32[]{:S(2)}, u32[]{:S(2)}) %collective-permute-start.12) | collective-permute-done | bytes 524320 | tf_op jit(solution)/shard_map/ppermute | solution.py:13
  322.2 0.9 fusion.113
  323.8 4.5 multiply_reduce_fusion.2
  328.3 1.4 collective-permute-start.13
  329.9 14.5 %collective-permute-done.13 = bf16[1,64,2048]{2,1,0:T(8,128)(2,1)S(1)} collective-permute-done((bf16[1,64,2048]{2,1,0:T(8,128)(2,1)S(1)}, bf16[1,64,2048]{2,1,0:T(8,128)(2,1)S(1)}, u32[]{:S(2)}, u32[]{:S(2)}) %collective-permute-start.13) | collective-permute-done | bytes 262176 | tf_op jit(solution)/shard_map/ppermute | solution.py:13
  345.9 1.4 collective-permute-start.14
  347.4 9.2 %collective-permute-done.14 = bf16[1,32,2048]{2,1,0:T(8,128)(2,1)S(1)} collective-permute-done((bf16[1,32,2048]{2,1,0:T(8,128)(2,1)S(1)}, bf16[1,32,2048]{2,1,0:T(8,128)(2,1)S(1)}, u32[]{:S(2)}, u32[]{:S(2)}) %collective-permute-start.14) | collective-permute-done | bytes 131104 | tf_op jit(solution)/shard_map/ppermute | solution.py:13
  357.6 3.8 multiply_reduce_fusion.4
  361.4 1.4 collective-permute-start.15
  362.9 6.9 %collective-permute-done.15 = bf16[1,16,2048]{2,1,0:T(8,128)(2,1)S(1)} collective-permute-done((bf16[1,16,2048]{2,1,0:T(8,128)(2,1)S(1)}, bf16[1,16,2048]{2,1,0:T(8,128)(2,1)S(1)}, u32[]{:S(2)}, u32[]{:S(2)}) %collective-permute-start.15) | collective-permute-done | bytes 65568 | tf_op jit(solution)/shard_map/ppermute | solution.py:13
  371.3 1.5 collective-permute-start.16
  372.9 5.4 %collective-permute-done.16 = bf16[1,8,2048]{2,1,0:T(8,128)(2,1)S(1)} collective-permute-done((bf16[1,8,2048]{2,1,0:T(8,128)(2,1)S(1)}, bf16[1,8,2048]{2,1,0:T(8,128)(2,1)S(1)}, u32[]{:S(2)}, u32[]{:S(2)}) %collective-permute-start.16) | collective-permute-done | bytes 32800 | tf_op jit(solution)/shard_map/ppermute | solution.py:13
  378.3 1.0 fusion.145
  379.3 4.1 multiply_reduce_fusion.6
  383.4 1.4 collective-permute-start.17
  385.1 4.8 %collective-permute-done.17 = bf16[1,4,2048]{2,1,0:T(4,128)(2,1)S(1)} collective-permute-done((bf16[1,4,2048]{2,1,0:T(4,128)(2,1)S(1)}, bf16[1,4,2048]{2,1,0:T(4,128)(2,1)S(1)}, u32[]{:S(2)}, u32[]{:S(2)}) %collective-permute-start.17) | collective-permute-done | bytes 16416 | tf_op jit(solution)/shard_map/ppermute | solution.py:13
  389.9 1.1 fusion.153
  391.5 1.4 collective-permute-start.18
  393.2 4.4 collective-permute-done.18
  397.7 2.0 fusion.161
  400.0 7.0 %multiply_reduce_fusion.8 = (f32[2048]{0:T(1024)}, f32[2048]{0:T(1024)}, f32[2048]{0:T(1024)}, f32[2048]{0:T(1024)}, f32[2048]{0:T(1024)}, /*index=5*/f32[2048]{...) fusion(f32[1,256,2048]{2,1,0:T(8,128)S(1)} %get-tuple-element.155, ...), kind=kLoop, calls=%fused_computation.295 | loop fusion | flops 25149440 | bytes 11641344 | tf_op jit(solution)/shard_map/reduce_sum | solution.py:111
  407.1 1.0 copy-done.33
  408.6 1.3 collective-permute-start.19
  409.9 1.7 stack.73
  412.5 14.0 %all_gather.8 = bf16[8,2,2048]{2,1,0:T(2,128)(2,1)S(1)} all-gather(bf16[1,2,2048]{2,1,0:T(2,128)(2,1)S(1)} %fusion.169), channel_id=1, replica_groups=mesh['groups'=2,'seq'=4,'tensor'=2,'dp'=2] {'seq','dp'}, dimensions={0}, use_global_device_ids=true | all-gather | bytes 73728 | tf_op jit(solution)/shard_map/all_gather | solution.py:139
  428.2 29.3 %all-reduce = (bf16[2,2048]{1,0:T(2,128)(2,1)S(1)}, bf16[13,2048]{1,0:T(8,128)(2,1)S(1)}) all-reduce(bf16[2,2048]{1,0:T(2,128)(2,1)S(1)} %fusion.170, bf16[13,2048]{1,0:T(8,128)(2,1)S(1)} %multiply_convert_fusion.3), channel_id=1, replica_groups=mesh['groups'=2,'seq'=4,'tensor'=2,'dp'=2] {'seq','dp'}, use_global_device_ids=true, to_apply=%region_53.54 | all-reduce | flops 30720 | bytes 122880 | tf_op jit(solution)/shard_map/psum | solution.py:142
  457.4 2.5 slice.349
  461.9 3.2 add_convert_fusion
  465.1 3.9 copy.15
  (352 shorter events, 21.1 us)
Async XLA Ops:
  7.2 149.4 %all-gather.2.cloned.1.call-start = ((), (), s32[]{:S(2)}) async-start(), calls=%async_computation.3 | async-start | bytes 3145728 | tf_op jit(solution)/shard_map/all_gather | solution.py:86
  8.0 8.0 %collective-permute-start = (bf16[1,1,2048]{2,1,0:T(2,128)(2,1)S(1)}, bf16[1,1,2048]{2,1,0:T(2,128)(2,1)S(1)}, u32[]{:S(2)}, u32[]{:S(2)}) collective-permute-start(bf16[1,1,2048]{2,1,0:T(2,128)(2,1)S(1)} %slice.100), channel_id=1, source_target_pairs={{0,4},{4,8},{8,12},{1,5},{5,9},{9,13},{2,6},{6,10},{10,14},{3,7},{... | collective-permute-start | bytes 12296 | tf_op jit(solution)/shard_map/ppermute | solution.py:13
  16.0 46.4 %copy-start.132 = (pred[256]{0:T(512)(128)(4,1)}, pred[256]{0:T(512)(128)(4,1)S(1)}, u32[]{:S(2)}) copy-start(pred[256]{0:T(512)(128)(4,1)S(1)} %get-tuple-element.147) | copy-start | bytes 772
  16.0 60.2 %copy-start.120 = (pred[256]{0:T(512)(128)(4,1)}, pred[256]{0:T(512)(128)(4,1)S(1)}, u32[]{:S(2)}) copy-start(pred[256]{0:T(512)(128)(4,1)S(1)} %get-tuple-element.146) | copy-start | bytes 772
  18.3 111.4 %copy-start = (bf16[1,256,2048]{2,1,0:T(8,128)(2,1)}, bf16[1,256,2048]{2,1,0:T(8,128)(2,1)S(1)}, u32[]{:S(2)}) copy-start(bf16[1,256,2048]{2,1,0:T(8,128)(2,1)S(1)} %fusion.18) | copy-start | bytes 3145732
  18.3 4.8 %collective-permute-start.1 = (bf16[1,2,2048]{2,1,0:T(2,128)(2,1)S(1)}, bf16[1,2,2048]{2,1,0:T(2,128)(2,1)S(1)}, u32[]{:S(2)}, u32[]{:S(2)}) collective-permute-start(bf16[1,2,2048]{2,1,0:T(2,128)(2,1)S(1)} %slice.147), channel_id=1, source_target_pairs={{0,4},{4,8},{8,12},{1,5},{5,9},{9,13},{2,6},{6,10},{10,14},{3,7},{... | collective-permute-start | bytes 24584 | tf_op jit(solution)/shard_map/ppermute | solution.py:13
  23.9 5.6 %collective-permute-start.2 = (bf16[1,4,2048]{2,1,0:T(4,128)(2,1)S(1)}, bf16[1,4,2048]{2,1,0:T(4,128)(2,1)S(1)}, u32[]{:S(2)}, u32[]{:S(2)}) collective-permute-start(bf16[1,4,2048]{2,1,0:T(4,128)(2,1)S(1)} %slice.149), channel_id=1, source_target_pairs={{0,4},{4,8},{8,12},{1,5},{5,9},{9,13},{2,6},{6,10},{10,14},{3,7},{... | collective-permute-start | bytes 49160 | tf_op jit(solution)/shard_map/ppermute | solution.py:13
  30.3 5.8 %collective-permute-start.3 = (bf16[1,8,2048]{2,1,0:T(8,128)(2,1)S(1)}, bf16[1,8,2048]{2,1,0:T(8,128)(2,1)S(1)}, u32[]{:S(2)}, u32[]{:S(2)}) collective-permute-start(bf16[1,8,2048]{2,1,0:T(8,128)(2,1)S(1)} %slice.151), channel_id=1, source_target_pairs={{0,4},{4,8},{8,12},{1,5},{5,9},{9,13},{2,6},{6,10},{10,14},{3,7},{... | collective-permute-start | bytes 98312 | tf_op jit(solution)/shard_map/ppermute | solution.py:13
  36.7 6.1 %collective-permute-start.4 = (bf16[1,16,2048]{2,1,0:T(8,128)(2,1)S(1)}, bf16[1,16,2048]{2,1,0:T(8,128)(2,1)S(1)}, u32[]{:S(2)}, u32[]{:S(2)}) collective-permute-start(bf16[1,16,2048]{2,1,0:T(8,128)(2,1)S(1)} %slice.153), channel_id=1, source_target_pairs={{0,4},{4,8},{8,12},{1,5},{5,9},{9,13},{2,6},{6,10},{10,14},{3,7},{... | collective-permute-start | bytes 196616 | tf_op jit(solution)/shard_map/ppermute | solution.py:13
  43.4 7.8 %collective-permute-start.5 = (bf16[1,32,2048]{2,1,0:T(8,128)(2,1)S(1)}, bf16[1,32,2048]{2,1,0:T(8,128)(2,1)S(1)}, u32[]{:S(2)}, u32[]{:S(2)}) collective-permute-start(bf16[1,32,2048]{2,1,0:T(8,128)(2,1)S(1)} %slice.155), channel_id=1, source_target_pairs={{0,4},{4,8},{8,12},{1,5},{5,9},{9,13},{2,6},{6,10},{10,14},{3,7},{... | collective-permute-start | bytes 393224 | tf_op jit(solution)/shard_map/ppermute | solution.py:13
  51.8 10.5 %collective-permute-start.6 = (bf16[1,64,2048]{2,1,0:T(8,128)(2,1)S(1)}, bf16[1,64,2048]{2,1,0:T(8,128)(2,1)S(1)}, u32[]{:S(2)}, u32[]{:S(2)}) collective-permute-start(bf16[1,64,2048]{2,1,0:T(8,128)(2,1)S(1)} %slice.157), channel_id=1, source_target_pairs={{0,4},{4,8},{8,12},{1,5},{5,9},{9,13},{2,6},{6,10},{10,14},{3,7},{... | collective-permute-start | bytes 786440 | tf_op jit(solution)/shard_map/ppermute | solution.py:13
  63.0 13.2 %collective-permute-start.7 = (bf16[1,128,2048]{2,1,0:T(8,128)(2,1)S(1)}, bf16[1,128,2048]{2,1,0:T(8,128)(2,1)S(1)}, u32[]{:S(2)}, u32[]{:S(2)}) collective-permute-start(bf16[1,128,2048]{2,1,0:T(8,128)(2,1)S(1)} %get-tuple-element.125), channel_id=1, source_target_pairs={{0,4},{4,8},{8,12},{1,5},{5,9},{9,13},{2,6},{6,10},{10,14},{3,7},{... | collective-permute-start | bytes 1572872 | tf_op jit(solution)/shard_map/ppermute | solution.py:13
  77.7 52.0 %copy-start.2 = (bf16[1,256,2048]{2,1,0:T(8,128)(2,1)S(1)}, bf16[1,256,2048]{2,1,0:T(8,128)(2,1)}, u32[]{:S(2)}) copy-start(bf16[1,256,2048]{2,1,0:T(8,128)(2,1)} %param.7) | copy-start | bytes 3145732
  77.7 20.4 %collective-permute-start.8 = (bf16[1,256,2048]{2,1,0:T(8,128)(2,1)}, bf16[1,256,2048]{2,1,0:T(8,128)(2,1)}, u32[]{:S(2)}, u32[]{:S(2)}) collective-permute-start(bf16[1,256,2048]{2,1,0:T(8,128)(2,1)} %fusion.52), channel_id=1, source_target_pairs={{0,4},{4,8},{8,12},{1,5},{5,9},{9,13},{2,6},{6,10},{10,14},{3,7},{... | collective-permute-start | bytes 3145736 | tf_op jit(solution)/shard_map/ppermute | solution.py:13
  83.3 316.4 %reduce-scatter.3.cloned.1.call-start = ((), (), s32[]{:S(2)}) async-start(), calls=%async_computation.2 | async-start | bytes 3145728 | tf_op jit(solution)/shard_map/reduce_scatter | solution.py:82
  83.4 46.3 %copy-start.5 = (bf16[1,256,2048]{2,1,0:T(8,128)(2,1)S(1)}, bf16[1,256,2048]{2,1,0:T(8,128)(2,1)}, u32[]{:S(2)}) copy-start(bf16[1,256,2048]{2,1,0:T(8,128)(2,1)} %copy-done.4) | copy-start | bytes 3145732
  83.4 46.3 %copy-start.8 = (bf16[1,256,2048]{2,1,0:T(8,128)(2,1)S(1)}, bf16[1,256,2048]{2,1,0:T(8,128)(2,1)}, u32[]{:S(2)}) copy-start(bf16[1,256,2048]{2,1,0:T(8,128)(2,1)} %copy-done.7) | copy-start | bytes 3145732
  83.4 46.3 %copy-start.11 = (bf16[1,256,2048]{2,1,0:T(8,128)(2,1)S(1)}, bf16[1,256,2048]{2,1,0:T(8,128)(2,1)}, u32[]{:S(2)}) copy-start(bf16[1,256,2048]{2,1,0:T(8,128)(2,1)} %copy-done.10) | copy-start | bytes 3145732
  83.4 46.3 %copy-start.45 = (bf16[1,16,2048]{2,1,0:T(8,128)(2,1)S(1)}, bf16[1,16,2048]{2,1,0:T(8,128)(2,1)}, u32[]{:S(2)}) copy-start(bf16[1,16,2048]{2,1,0:T(8,128)(2,1)} %copy-done.44) | copy-start | bytes 196612
  83.4 46.3 %copy-start.48 = (bf16[1,8,2048]{2,1,0:T(8,128)(2,1)S(1)}, bf16[1,8,2048]{2,1,0:T(8,128)(2,1)}, u32[]{:S(2)}) copy-start(bf16[1,8,2048]{2,1,0:T(8,128)(2,1)} %copy-done.47) | copy-start | bytes 98308
  83.4 46.3 %copy-start.51 = (bf16[1,4,2048]{2,1,0:T(4,128)(2,1)S(1)}, bf16[1,4,2048]{2,1,0:T(4,128)(2,1)}, u32[]{:S(2)}) copy-start(bf16[1,4,2048]{2,1,0:T(4,128)(2,1)} %copy-done.50) | copy-start | bytes 49156
  83.4 46.3 %copy-start.64 = (bf16[1,1,2048]{2,1,0:T(2,128)(2,1)S(1)}, bf16[1,1,2048]{2,1,0:T(2,128)(2,1)}, u32[]{:S(2)}) copy-start(bf16[1,1,2048]{2,1,0:T(2,128)(2,1)} %copy-done.63) | copy-start | bytes 12292
  83.4 46.3 %copy-start.67 = (bf16[1,2,2048]{2,1,0:T(2,128)(2,1)S(1)}, bf16[1,2,2048]{2,1,0:T(2,128)(2,1)}, u32[]{:S(2)}) copy-start(bf16[1,2,2048]{2,1,0:T(2,128)(2,1)} %copy-done.66) | copy-start | bytes 24580
  83.4 46.3 %copy-start.115 = (pred[256]{0:T(512)(128)(4,1)S(1)}, pred[256]{0:T(512)(128)(4,1)}, u32[]{:S(2)}) copy-start(pred[256]{0:T(512)(128)(4,1)} %copy-done.114) | copy-start | bytes 772
  83.5 46.3 %copy-start.118 = (pred[256]{0:T(512)(128)(4,1)S(1)}, pred[256]{0:T(512)(128)(4,1)}, u32[]{:S(2)}) copy-start(pred[256]{0:T(512)(128)(4,1)} %copy-done.117) | copy-start | bytes 772
  83.5 46.3 %copy-start.121 = (pred[256]{0:T(512)(128)(4,1)S(1)}, pred[256]{0:T(512)(128)(4,1)}, u32[]{:S(2)}) copy-start(pred[256]{0:T(512)(128)(4,1)} %copy-done.120) | copy-start | bytes 772
  83.5 46.3 %copy-start.124 = (pred[256]{0:T(512)(128)(4,1)S(1)}, pred[256]{0:T(512)(128)(4,1)}, u32[]{:S(2)}) copy-start(pred[256]{0:T(512)(128)(4,1)} %copy-done.123) | copy-start | bytes 772
  83.5 46.3 %copy-start.127 = (pred[256]{0:T(512)(128)(4,1)S(1)}, pred[256]{0:T(512)(128)(4,1)}, u32[]{:S(2)}) copy-start(pred[256]{0:T(512)(128)(4,1)} %copy-done.126) | copy-start | bytes 772
  83.5 46.3 %copy-start.130 = (pred[256]{0:T(512)(128)(4,1)S(1)}, pred[256]{0:T(512)(128)(4,1)}, u32[]{:S(2)}) copy-start(pred[256]{0:T(512)(128)(4,1)} %copy-done.129) | copy-start | bytes 772
  83.5 46.3 %copy-start.133 = (pred[256]{0:T(512)(128)(4,1)S(1)}, pred[256]{0:T(512)(128)(4,1)}, u32[]{:S(2)}) copy-start(pred[256]{0:T(512)(128)(4,1)} %copy-done.132) | copy-start | bytes 772
  83.5 46.3 %copy-start.135 = (pred[256]{0:T(512)(128)(4,1)S(1)}, pred[256]{0:T(512)(128)(4,1)}, u32[]{:S(2)}) copy-start(pred[256]{0:T(512)(128)(4,1)} %get-tuple-element.145) | copy-start | bytes 772
  83.5 46.3 %copy-start.138 = (pred[256]{0:T(512)(128)(4,1)S(1)}, pred[256]{0:T(512)(128)(4,1)}, u32[]{:S(2)}) copy-start(pred[256]{0:T(512)(128)(4,1)} %copy-done.137) | copy-start | bytes 772
  83.5 46.3 %copy-start.140 = (pred[256]{0:T(512)(128)(4,1)S(1)}, pred[256]{0:T(512)(128)(4,1)}, u32[]{:S(2)}) copy-start(pred[256]{0:T(512)(128)(4,1)} %get-tuple-element.144) | copy-start | bytes 772
  100.2 29.5 %collective-permute-start.9 = (bf16[1,256,2048]{2,1,0:T(8,128)(2,1)S(1)}, bf16[1,256,2048]{2,1,0:T(8,128)(2,1)S(1)}, u32[]{:S(2)}, u32[]{:S(2)}) collective-permute-start(bf16[1,256,2048]{2,1,0:T(8,128)(2,1)S(1)} %fusion.57), channel_id=1, source_target_pairs={{0,8},{4,12},{1,9},{5,13},{2,10},{6,14},{3,11},{7,15},{16,24},{20,... | collective-permute-start | bytes 3145736 | tf_op jit(solution)/shard_map/ppermute | solution.py:13
  156.3 308.8 %reduce-scatter.5.cloned.1.call-start = ((), (), s32[]{:S(2)}) async-start(), calls=%async_computation.4 | async-start | bytes 18874368 | tf_op jit(solution)/shard_map/reduce_scatter | solution.py:88
  167.9 66.6 %copy-start.29 = (bf16[1,256,2048]{2,1,0:T(8,128)(2,1)S(1)}, bf16[1,256,2048]{2,1,0:T(8,128)(2,1)}, u32[]{:S(2)}) copy-start(bf16[1,256,2048]{2,1,0:T(8,128)(2,1)} %copy-done.28) | copy-start | bytes 3145732
  167.9 66.6 %copy-start.35 = (bf16[1,256,2048]{2,1,0:T(8,128)(2,1)S(1)}, bf16[1,256,2048]{2,1,0:T(8,128)(2,1)}, u32[]{:S(2)}) copy-start(bf16[1,256,2048]{2,1,0:T(8,128)(2,1)} %copy-done.34) | copy-start | bytes 3145732
  167.9 66.6 %copy-start.36 = (bf16[1,256,2048]{2,1,0:T(8,128)(2,1)S(1)}, bf16[1,256,2048]{2,1,0:T(8,128)(2,1)}, u32[]{:S(2)}) copy-start(bf16[1,256,2048]{2,1,0:T(8,128)(2,1)} %get-tuple-element.117) | copy-start | bytes 3145732
  168.0 66.6 %copy-start.39 = (f32[1,2048]{1,0:T(1,128)S(1)}, f32[1,2048]{1,0:T(1,128)}, u32[]{:S(2)}) copy-start(f32[1,2048]{1,0:T(1,128)} %copy-done.38) | copy-start | bytes 24580
  168.0 66.6 %copy-start.42 = (f32[1,2048]{1,0:T(1,128)S(1)}, f32[1,2048]{1,0:T(1,128)}, u32[]{:S(2)}) copy-start(f32[1,2048]{1,0:T(1,128)} %copy-done.41) | copy-start | bytes 24580
  168.0 66.6 %copy-start.62 = (f32[1,2048]{1,0:T(1,128)S(1)}, f32[1,2048]{1,0:T(1,128)}, u32[]{:S(2)}) copy-start(f32[1,2048]{1,0:T(1,128)} %copy-done.61) | copy-start | bytes 24580
  168.0 66.6 %copy-start.78 = (f32[2048]{0:T(1024)S(1)}, f32[2048]{0:T(1024)}, u32[]{:S(2)}) copy-start(f32[2048]{0:T(1024)} %copy-done.77) | copy-start | bytes 24580
  168.0 66.6 %copy-start.80 = (f32[2048]{0:T(1024)S(1)}, f32[2048]{0:T(1024)}, u32[]{:S(2)}) copy-start(f32[2048]{0:T(1024)} %copy-done.79) | copy-start | bytes 24580
  168.0 66.6 %copy-start.82 = (f32[1,2048]{1,0:T(1,128)S(1)}, f32[1,2048]{1,0:T(1,128)}, u32[]{:S(2)}) copy-start(f32[1,2048]{1,0:T(1,128)} %copy-done.81) | copy-start | bytes 24580
  168.0 66.6 %copy-start.84 = (f32[1,2048]{1,0:T(1,128)S(1)}, f32[1,2048]{1,0:T(1,128)}, u32[]{:S(2)}) copy-start(f32[1,2048]{1,0:T(1,128)} %copy-done.83) | copy-start | bytes 24580
  168.0 66.6 %copy-start.86 = (f32[1,2048]{1,0:T(1,128)S(1)}, f32[1,2048]{1,0:T(1,128)}, u32[]{:S(2)}) copy-start(f32[1,2048]{1,0:T(1,128)} %copy-done.85) | copy-start | bytes 24580
  168.0 66.6 %copy-start.88 = (f32[1,2048]{1,0:T(1,128)S(1)}, f32[1,2048]{1,0:T(1,128)}, u32[]{:S(2)}) copy-start(f32[1,2048]{1,0:T(1,128)} %copy-done.87) | copy-start | bytes 24580
  168.1 66.6 %copy-start.136 = (pred[256]{0:T(512)(128)(4,1)S(1)}, pred[256]{0:T(512)(128)(4,1)}, u32[]{:S(2)}) copy-start(pred[256]{0:T(512)(128)(4,1)} %get-tuple-element.145) | copy-start | bytes 772
  168.1 66.6 %copy-start.141 = (pred[256]{0:T(512)(128)(4,1)S(1)}, pred[256]{0:T(512)(128)(4,1)}, u32[]{:S(2)}) copy-start(pred[256]{0:T(512)(128)(4,1)} %get-tuple-element.144) | copy-start | bytes 772
  179.2 55.3 %collective-permute-start.10 = (bf16[1,256,2048]{2,1,0:T(8,128)(2,1)S(1)}, bf16[1,256,2048]{2,1,0:T(8,128)(2,1)S(1)}, u32[]{:S(2)}, u32[]{:S(2)}) collective-permute-start(bf16[1,256,2048]{2,1,0:T(8,128)(2,1)S(1)} %get-tuple-element.154), channel_id=1, source_target_pairs={{8,0},{12,4},{9,1},{13,5},{10,2},{14,6},{11,3},{15,7},{24,16},{28,... | collective-permute-start | bytes 3145736 | tf_op jit(solution)/shard_map/ppermute | solution.py:13
  243.1 50.8 %copy-start.27 = (bf16[1,128,2048]{2,1,0:T(8,128)(2,1)S(1)}, bf16[1,128,2048]{2,1,0:T(8,128)(2,1)}, u32[]{:S(2)}) copy-start(bf16[1,128,2048]{2,1,0:T(8,128)(2,1)} %copy-done.26) | copy-start | bytes 1572868
  243.1 50.8 %copy-start.32 = (bf16[1,128,2048]{2,1,0:T(8,128)(2,1)S(1)}, bf16[1,128,2048]{2,1,0:T(8,128)(2,1)}, u32[]{:S(2)}) copy-start(bf16[1,128,2048]{2,1,0:T(8,128)(2,1)} %copy-done.31) | copy-start | bytes 1572868
  243.1 50.8 %copy-start.122 = (pred[256]{0:T(512)(128)(4,1)S(1)}, pred[256]{0:T(512)(128)(4,1)}, u32[]{:S(2)}) copy-start(pred[256]{0:T(512)(128)(4,1)} %copy-done.120) | copy-start | bytes 772
  243.6 51.3 %copy-start.60 = (f32[1,2048]{1,0:T(1,128)S(1)}, f32[1,2048]{1,0:T(1,128)}, u32[]{:S(2)}) copy-start(f32[1,2048]{1,0:T(1,128)} %copy-done.59) | copy-start | bytes 24580
  243.6 50.3 %collective-permute-start.11 = (bf16[1,256,2048]{2,1,0:T(8,128)(2,1)S(1)}, bf16[1,256,2048]{2,1,0:T(8,128)(2,1)S(1)}, u32[]{:S(2)}, u32[]{:S(2)}) collective-permute-start(bf16[1,256,2048]{2,1,0:T(8,128)(2,1)S(1)} %fusion.96), channel_id=1, source_target_pairs={{4,0},{8,4},{12,8},{5,1},{9,5},{13,9},{6,2},{10,6},{14,10},{7,3},{... | collective-permute-start | bytes 3145736 | tf_op jit(solution)/shard_map/ppermute | solution.py:13
  295.5 26.7 %collective-permute-start.12 = (bf16[1,128,2048]{2,1,0:T(8,128)(2,1)S(1)}, bf16[1,128,2048]{2,1,0:T(8,128)(2,1)S(1)}, u32[]{:S(2)}, u32[]{:S(2)}) collective-permute-start(bf16[1,128,2048]{2,1,0:T(8,128)(2,1)S(1)} %get-tuple-element.124), channel_id=1, source_target_pairs={{4,0},{8,4},{12,8},{5,1},{9,5},{13,9},{6,2},{10,6},{14,10},{7,3},{... | collective-permute-start | bytes 1572872 | tf_op jit(solution)/shard_map/ppermute | solution.py:13
  328.3 16.1 %collective-permute-start.13 = (bf16[1,64,2048]{2,1,0:T(8,128)(2,1)S(1)}, bf16[1,64,2048]{2,1,0:T(8,128)(2,1)S(1)}, u32[]{:S(2)}, u32[]{:S(2)}) collective-permute-start(bf16[1,64,2048]{2,1,0:T(8,128)(2,1)S(1)} %slice.164), channel_id=1, source_target_pairs={{4,0},{8,4},{12,8},{5,1},{9,5},{13,9},{6,2},{10,6},{14,10},{7,3},{... | collective-permute-start | bytes 786440 | tf_op jit(solution)/shard_map/ppermute | solution.py:13
  345.9 10.7 %collective-permute-start.14 = (bf16[1,32,2048]{2,1,0:T(8,128)(2,1)S(1)}, bf16[1,32,2048]{2,1,0:T(8,128)(2,1)S(1)}, u32[]{:S(2)}, u32[]{:S(2)}) collective-permute-start(bf16[1,32,2048]{2,1,0:T(8,128)(2,1)S(1)} %slice.166), channel_id=1, source_target_pairs={{4,0},{8,4},{12,8},{5,1},{9,5},{13,9},{6,2},{10,6},{14,10},{7,3},{... | collective-permute-start | bytes 393224 | tf_op jit(solution)/shard_map/ppermute | solution.py:13
  361.4 8.4 %collective-permute-start.15 = (bf16[1,16,2048]{2,1,0:T(8,128)(2,1)S(1)}, bf16[1,16,2048]{2,1,0:T(8,128)(2,1)S(1)}, u32[]{:S(2)}, u32[]{:S(2)}) collective-permute-start(bf16[1,16,2048]{2,1,0:T(8,128)(2,1)S(1)} %slice.168), channel_id=1, source_target_pairs={{4,0},{8,4},{12,8},{5,1},{9,5},{13,9},{6,2},{10,6},{14,10},{7,3},{... | collective-permute-start | bytes 196616 | tf_op jit(solution)/shard_map/ppermute | solution.py:13
  371.3 7.0 %collective-permute-start.16 = (bf16[1,8,2048]{2,1,0:T(8,128)(2,1)S(1)}, bf16[1,8,2048]{2,1,0:T(8,128)(2,1)S(1)}, u32[]{:S(2)}, u32[]{:S(2)}) collective-permute-start(bf16[1,8,2048]{2,1,0:T(8,128)(2,1)S(1)} %slice.170), channel_id=1, source_target_pairs={{4,0},{8,4},{12,8},{5,1},{9,5},{13,9},{6,2},{10,6},{14,10},{7,3},{... | collective-permute-start | bytes 98312 | tf_op jit(solution)/shard_map/ppermute | solution.py:13
  383.4 6.5 %collective-permute-start.17 = (bf16[1,4,2048]{2,1,0:T(4,128)(2,1)S(1)}, bf16[1,4,2048]{2,1,0:T(4,128)(2,1)S(1)}, u32[]{:S(2)}, u32[]{:S(2)}) collective-permute-start(bf16[1,4,2048]{2,1,0:T(4,128)(2,1)S(1)} %slice.172), channel_id=1, source_target_pairs={{4,0},{8,4},{12,8},{5,1},{9,5},{13,9},{6,2},{10,6},{14,10},{7,3},{... | collective-permute-start | bytes 49160 | tf_op jit(solution)/shard_map/ppermute | solution.py:13
  391.5 6.1 %collective-permute-start.18 = (bf16[1,2,2048]{2,1,0:T(2,128)(2,1)S(1)}, bf16[1,2,2048]{2,1,0:T(2,128)(2,1)S(1)}, u32[]{:S(2)}, u32[]{:S(2)}) collective-permute-start(bf16[1,2,2048]{2,1,0:T(2,128)(2,1)S(1)} %slice.348), channel_id=1, source_target_pairs={{4,0},{8,4},{12,8},{5,1},{9,5},{13,9},{6,2},{10,6},{14,10},{7,3},{... | collective-permute-start | bytes 24584 | tf_op jit(solution)/shard_map/ppermute | solution.py:13
  407.1 54.8 %copy-start.30 = (bf16[1,256,2048]{2,1,0:T(8,128)(2,1)S(1)}, bf16[1,256,2048]{2,1,0:T(8,128)(2,1)}, u32[]{:S(2)}) copy-start(bf16[1,256,2048]{2,1,0:T(8,128)(2,1)} %get-tuple-element.114) | copy-start | bytes 3145732
  408.6 53.2 %collective-permute-start.19 = (bf16[1,1,2048]{2,1,0:T(2,128)(2,1)}, bf16[1,1,2048]{2,1,0:T(2,128)(2,1)}, u32[]{:S(2)}, u32[]{:S(2)}) collective-permute-start(bf16[1,1,2048]{2,1,0:T(2,128)(2,1)} %slice.350), channel_id=1, source_target_pairs={{4,0},{8,4},{12,8},{5,1},{9,5},{13,9},{6,2},{10,6},{14,10},{7,3},{... | collective-permute-start | bytes 12296 | tf_op jit(solution)/shard_map/ppermute | solution.py:13
  (101 other events, 1520.3 us)
Sparse Core Ops, SparseCore 0:
  83.4 32.3 all-gather.1
  156.4 45.6 reduce-scatter.2
  204.6 213.2 reduce-scatter.4
